TPU v7x, 256 devices: a whole 4x4x8 slice. The times are simulated.
256 devices in a mesh: rep: 64 (over y, x, z_lo), slab: 4 (over z_hi, core).
Axes of the slice: x: 4, y: 4, z: 8 (z_hi: 2, z_lo: 4; z = z_hi * 4 + z_lo), core: 2. Of those that a mesh axis runs over, the one named last changes fastest.
Arguments:
- positions: float32 [64, 3, 16384], P('rep', None, 'slab'), may hold values from 0 to 2
- velocities: float32 [64, 3, 16384], P('rep', None, 'slab'), may hold values from -6 to 6
- inv_mass: float32 [16384], P('slab'), may hold values from 0.5 to 2
- strength: float32 [16384], P('slab'), may hold values from 0.5 to 2
- charge: float32 [16384], P('slab'), may hold values from -1 to 1
- scaling: float32 [64], P('rep'), may hold values from 0.3 to 1
- tile_pairs: int32 [64, 2, 768], P('rep', None, 'slab'), may hold values from 0 to 79, as said below
- tile_counts: int32 [64, 4], P('rep', 'slab'), may hold values from 24 to 192, as said below
- halo_clusters: int32 [64, 64], P('rep', 'slab'), may hold values from 0 to 63, as said below
- swap_pairs: int32 [16, 2], replicated, may hold values from 0 to 63, as said below
Outputs:
- new_positions: float32 [64, 3, 16384], P('rep', None, 'slab')
- new_velocities: float32 [64, 3, 16384], P('rep', None, 'slab')
- potential: float32 [64], P('rep')
Inputs may be any that keep to these rules, and one draw needn't show every extreme that they name: `tile_pairs`: for each replica and slab, the 192 columns are distinct tiles (i, j) with i a cluster of that slab and i <= j; j below 64 is a cluster of the same slab, j = 64 + h is halo slot h. Only the first tile_counts columns are live. `tile_counts`: in every replica some slab has all 192 tiles live. `halo_clusters`: the 16 clusters of each replica and slab are distinct. `swap_pairs`: no replica appears twice. The first pair joins two replicas 64 // 2 apart (counted round), the second two neighbouring replicas (counted round); the others are arbitrary.
All inputs are finite; a program needn't handle non-finite values.
Results may differ from a plain program's by a relative error of at most 0.0003.
Values sent between devices are 32-bit elements; how exact they have to be, the bound alone decides.
No kernel may reach another device: no remote copies, remote signals or barrier semaphores. Data moves between devices by JAX's collectives and lax.ppermute only.
A program may use at most 64 MiB of HBM per device.

v0:
```python
import jax
import jax.numpy as jnp
from jax import lax
from jax.sharding import PartitionSpec as P

CL = 64
CD = 64
STEPS = 4
HALO = 16
NT_MAX = 192
tile_block = 16
time_step = 0.04
half_step = 0.02
soft_sq = 0.25
slab_width = 2.0
exact = lax.Precision.HIGHEST


def from_behind(value, axis, steps):
    count = lax.axis_size(axis)
    pairs = [(source, (source + steps) % count) for source in range(count)]
    return lax.ppermute(value, axis, pairs)


def partner_of(pair_list, replica_ids):
    first_col = pair_list[:, 0]
    second_col = pair_list[:, 1]
    hit_first = replica_ids[:, None] == first_col[None, :]
    hit_second = replica_ids[:, None] == second_col[None, :]
    partner_sum = jnp.sum(jnp.where(hit_first, second_col[None, :], 0), 1) + jnp.sum(
        jnp.where(hit_second, first_col[None, :], 0), 1
    )
    listed = jnp.any(hit_first, 1) | jnp.any(hit_second, 1)
    return jnp.where(listed, partner_sum, replica_ids)


def select_table(index_list, width):
    cluster_ids = jnp.arange(width, dtype=jnp.int32)
    return (index_list[:, None] == cluster_ids[None, :]).astype(jnp.float32)


def pair_block(extended, strength_all, charge_all, ham_scale, tile_first, tile_second, live_mask):
    count_tiles = tile_first.shape[0]
    width = extended.shape[1]
    select_first = select_table(tile_first, width)
    select_second = select_table(tile_second, width)
    coords_i = jnp.einsum("te,xec->xct", select_first, extended, precision=exact)
    coords_j = jnp.einsum("te,xec->xtc", select_second, extended, precision=exact)
    offsets = (coords_i[:, :, :, None] - coords_j[:, None, :, :]).reshape(3, CL, count_tiles * CL)
    sq_dist = offsets[0] * offsets[0] + offsets[1] * offsets[1] + offsets[2] * offsets[2]
    params_all = jnp.stack([strength_all, charge_all], 0)
    params_i = jnp.einsum("te,pec->pct", select_first, params_all, precision=exact)
    params_j = jnp.einsum("te,pec->ptc", select_second, params_all, precision=exact)
    strength_prod = (params_i[0][:, :, None] * params_j[0][None, :, :]).reshape(
        CL, count_tiles * CL
    )
    charge_prod = (params_i[1][:, :, None] * params_j[1][None, :, :]).reshape(CL, count_tiles * CL)
    gauss_term = strength_prod * jnp.exp(-sq_dist)
    inv_root = lax.rsqrt(sq_dist + soft_sq)
    coulomb = ham_scale * charge_prod * inv_root
    same_tile = tile_first == tile_second
    weight_tile = jnp.where(live_mask, jnp.where(same_tile, 0.5, 1.0), 0.0).astype(jnp.float32)
    weight_col = jnp.repeat(weight_tile, CL)[None, :]
    slope = gauss_term + 0.5 * coulomb * inv_root * inv_root
    pushes = (2.0 * slope * weight_col)[None, :, :] * offsets
    force_i = pushes.reshape(3, CL, count_tiles, CL).sum(-1)
    force_j = -pushes.sum(1).reshape(3, count_tiles, CL)
    atom_ids = jnp.arange(CL, dtype=jnp.int32)
    column_ids = jnp.arange(count_tiles * CL, dtype=jnp.int32) % CL
    self_pair = jnp.repeat(same_tile, CL)[None, :] & (atom_ids[:, None] == column_ids[None, :])
    energy = jnp.sum(jnp.where(self_pair, 0.0, (gauss_term + coulomb) * weight_col))
    spread_i = jnp.einsum("te,xct->xec", select_first, force_i, precision=exact)
    spread_j = jnp.einsum("te,xtc->xec", select_second, force_j, precision=exact)
    return (spread_i + spread_j, energy)


def local(
    positions,
    velocities,
    inv_mass,
    strength,
    charge,
    scaling,
    tile_pairs,
    tile_counts,
    halo_clusters,
    swap_pairs,
):
    coords = positions[0]
    speeds = velocities[0]
    ham_scale = scaling[0]
    firsts_flat = tile_pairs[0, 0]
    seconds_flat = tile_pairs[0, 1]
    live_count = tile_counts[0, 0]
    halo_index = halo_clusters[0]
    atoms_here = coords.shape[1]
    halo_table = select_table(halo_index, CD)
    params = jnp.stack([strength, charge], 0).reshape(2, CD, CL)
    sent_params = jnp.einsum("hc,pck->phk", halo_table, params, precision=exact).reshape(
        2, HALO * CL
    )
    got_params = from_behind(sent_params, "slab", -1).reshape(2, HALO, CL)
    strength_all = jnp.concatenate([params[0], got_params[0]], 0)
    charge_all = jnp.concatenate([params[1], got_params[1]], 0)
    lift = jnp.array([0.0, 0.0, slab_width], jnp.float32)[:, None]
    extended_now = [None]

    def add_block(totals, tile_first, tile_second, slot_row):
        spread, energy_part = pair_block(
            extended_now[0],
            strength_all,
            charge_all,
            ham_scale,
            tile_first,
            tile_second,
            slot_row < live_count,
        )
        return (totals[0] + spread, totals[1] + energy_part)

    def evaluate(coords_now):
        blocks = coords_now.reshape(3, CD, CL)
        sent_coords = jnp.einsum("hc,xck->xhk", halo_table, blocks, precision=exact).reshape(
            3, HALO * CL
        )
        from_above = from_behind(sent_coords, "slab", -1) + lift
        extended_now[0] = jnp.concatenate([blocks, from_above.reshape(3, HALO, CL)], 1)
        start_state = (jnp.zeros((3, CD + HALO, CL), jnp.float32), jnp.zeros((), jnp.float32))
        firsts = firsts_flat.reshape(-1, tile_block)
        seconds = seconds_flat.reshape(-1, tile_block)
        slot_ids = jnp.arange(NT_MAX, dtype=jnp.int32).reshape(-1, tile_block)

        def visit_block(totals, inputs):
            return (add_block(totals, inputs[0], inputs[1], inputs[2]), None)

        result, _ = lax.scan(visit_block, start_state, (firsts, seconds, slot_ids))
        forces, energy = result
        returned = from_behind(forces[:, CD:].reshape(3, HALO * CL), "slab", 1)
        back_home = jnp.einsum(
            "hc,xhk->xck", halo_table, returned.reshape(3, HALO, CL), precision=exact
        )
        local_forces = forces[:, :CD] + back_home
        return (local_forces.reshape(3, atoms_here), energy)

    forces, energy = evaluate(coords)
    for step_idx in range(STEPS):
        speeds = speeds + half_step * forces * inv_mass
        coords = coords + time_step * speeds
        forces, energy = evaluate(coords)
        speeds = speeds + half_step * forces * inv_mass
    total_energy = lax.psum(energy, "slab")
    potential = (total_energy / (atoms_here * lax.axis_size("slab"))).reshape(1)
    state = jnp.concatenate([coords, speeds], 0)
    partner_me = partner_of(swap_pairs, lax.axis_index("rep").reshape(1))[0]
    shard_rows = lax.all_gather(state[None], "rep", axis=0, tiled=True)
    row_ids = jnp.arange(shard_rows.shape[0], dtype=jnp.int32)
    chosen = row_ids == partner_me
    swapped = jnp.sum(jnp.where(chosen[:, None, None], shard_rows, 0.0), 0)
    return (swapped[:3][None], swapped[3:][None], potential)


def solution(mesh):
    in_specs = (
        P("rep", None, "slab"),
        P("rep", None, "slab"),
        P("slab"),
        P("slab"),
        P("slab"),
        P("rep"),
        P("rep", None, "slab"),
        P("rep", "slab"),
        P("rep", "slab"),
        P(),
    )
    out_specs = (P("rep", None, "slab"), P("rep", None, "slab"), P("rep"))
    return jax.shard_map(local, mesh=mesh, in_specs=in_specs, out_specs=out_specs, check_vma=False)
```

profile of v0, /device:TPU:0, one launch (start us, length us, event | category | flops | bytes accessed | tf_op | source)
XLA Modules:
  0.0 775.9 jit_solution(11839752525932202935)
XLA Ops:
  9.7 4.9 collective-permute-start
  21.1 60.0 %while.67 = (s32[]{:T(128)}, f32[3,80,64]{1,2,0:T(8,128)S(1)}, s32[12,16]{1,0:T(8,128)S(1)}, f32[2,80,64]{1,2,0:T(8,128)S(1)}, s32[12,16]{1,0:T(8,128)S(1)}, /*i...) while((s32[]{:T(128)}, f32[3,80,64]{1,2,0:T(8,128)S(1)}, ...), condition=%wide.region_7.8_spmd.clone, body=%wide.region_4.7_spmd.clone.sunk | while | flops 17876564 | bytes 2778059 | solution.py:135
  23.6 1.0 fusion.306
  28.6 1.0 fusion.306
  33.6 1.0 fusion.306
  38.6 1.0 fusion.306
  43.6 1.0 fusion.306
  48.6 1.0 fusion.306
  53.6 1.0 fusion.306
  58.6 1.0 fusion.306
  63.6 1.0 fusion.306
  68.6 1.0 fusion.306
  73.6 1.0 fusion.306
  78.6 1.0 fusion.306
  82.1 6.4 collective-permute-done.2
  89.3 1.4 collective-permute-done.3
  91.1 60.0 %while.68 = (s32[]{:T(128)}, f32[3,80,64]{1,2,0:T(8,128)S(1)}, s32[12,16]{1,0:T(8,128)S(1)}, f32[2,80,64]{1,2,0:T(8,128)S(1)}, s32[12,16]{1,0:T(8,128)S(1)}, /*i...) while((s32[]{:T(128)}, f32[3,80,64]{1,2,0:T(8,128)S(1)}, ...), condition=%wide.region_11.12_spmd.clone, body=%wide.region_8.11_spmd.clone.sunk | while | flops 17876564 | bytes 2778059 | solution.py:135
  108.6 1.0 fusion.322
  128.6 1.0 fusion.322
  148.6 1.0 fusion.322
  152.0 6.5 collective-permute-done.4
  159.5 1.4 collective-permute-done.5
  161.3 60.0 %while.69 = (s32[]{:T(128)}, f32[3,80,64]{1,2,0:T(8,128)S(1)}, s32[12,16]{1,0:T(8,128)S(1)}, f32[2,80,64]{1,2,0:T(8,128)S(1)}, s32[12,16]{1,0:T(8,128)S(1)}, /*i...) while((s32[]{:T(128)}, f32[3,80,64]{1,2,0:T(8,128)S(1)}, ...), condition=%wide.region_15.16_spmd.clone, body=%wide.region_12.15_spmd.clone.sunk | while | flops 17876564 | bytes 2778059 | solution.py:135
  168.8 1.0 fusion.338
  188.8 1.0 fusion.338
  208.8 1.0 fusion.338
  222.2 6.5 collective-permute-done.6
  229.5 1.4 collective-permute-done.7
  231.3 60.0 %while.70 = (s32[]{:T(128)}, f32[3,80,64]{1,2,0:T(8,128)S(1)}, s32[12,16]{1,0:T(8,128)S(1)}, f32[2,80,64]{1,2,0:T(8,128)S(1)}, s32[12,16]{1,0:T(8,128)S(1)}, /*i...) while((s32[]{:T(128)}, f32[3,80,64]{1,2,0:T(8,128)S(1)}, ...), condition=%wide.region_19.20_spmd.clone, body=%wide.region_16.19_spmd.clone.sunk | while | flops 17876564 | bytes 2778059 | solution.py:135
  292.1 6.5 collective-permute-done.8
  299.4 1.4 collective-permute-done.9
  301.2 77.0 %while.71 = (s32[]{:T(128)}, f32[3,80,64]{1,2,0:T(8,128)S(1)}, f32[]{:T(128)}, s32[12,16]{1,0:T(8,128)S(1)}, f32[2,80,64]{1,2,0:T(8,128)S(1)}, /*index=5*/s32[12...) while((s32[]{:T(128)}, f32[3,80,64]{1,2,0:T(8,128)S(1)}, ...), condition=%wide.region_24.25_spmd.clone, body=%wide.region_20.24_spmd.clone.sunk | while | flops 18283088 | bytes 2786435 | solution.py:135
  303.7 1.8 select_reduce_fusion.3
  310.1 1.8 select_reduce_fusion.3
  316.5 1.8 select_reduce_fusion.3
  323.0 1.8 select_reduce_fusion.3
  329.4 1.8 select_reduce_fusion.3
  335.8 1.8 select_reduce_fusion.3
  342.2 1.8 select_reduce_fusion.3
  348.6 1.8 select_reduce_fusion.3
  355.0 1.8 select_reduce_fusion.3
  361.5 1.8 select_reduce_fusion.3
  367.9 1.8 select_reduce_fusion.3
  374.3 1.8 select_reduce_fusion.3
  380.1 5.7 collective-permute-done.10
  391.2 10.9 %psum.7 = f32[]{:T(128)} all-reduce(f32[]{:T(128)} %get-tuple-element.598), channel_id=1, replica_groups=mesh['rep'=64,'slab'=4] {'slab'}, use_global_device_ids=true, to_apply=%region_26.27 | all-reduce | flops 1 | bytes 8 | tf_op jit(solution)/shard_map/psum | solution.py:150
  402.8 359.3 %all-gather.4.cloned.1.call-done = f32[64,6,4096]{2,1,0:T(8,128)} async-done(((f32[1,6,4096]{2,1,0:T(8,128)}), f32[64,6,4096]{2,1,0:T(8,128)}) %all-gather.4.cloned.1.call-update) | async-done | bytes 6291472 | tf_op jit(solution)/shard_map/all_gather | solution.py:154
  762.1 4.5 select_reduce_fusion.1
  (1011 shorter events, 287.0 us)
Async XLA Ops:
  7.2 754.9 %all-gather.4.cloned.1.call-start = ((), (), s32[]{:S(2)}) async-start(), calls=%async_computation | async-start | bytes 8519680 | tf_op jit(solution)/shard_map/all_gather | solution.py:154
  9.7 10.2 %collective-permute-start = (f32[2,1024]{1,0:T(2,128)S(1)}, f32[2,1024]{1,0:T(2,128)S(1)}, u32[]{:S(2)}, u32[]{:S(2)}) collective-permute-start(f32[2,1024]{1,0:T(2,128)S(1)} %reshape.1061), channel_id=1, source_target_pairs={{0,3},{1,0},{2,1},{3,2},{4,7},{5,4},{6,5},{7,6},{8,11},{9,8},{10,9... | collective-permute-start | bytes 24584 | tf_op jit(solution)/shard_map/ppermute | solution.py:22
  16.6 3.5 collective-permute-start.1
  21.1 60.4 %copy-start.3 = (f32[4096]{0:T(1024)S(1)}, f32[4096]{0:T(1024)}, u32[]{:S(2)}) copy-start(f32[4096]{0:T(1024)} %param.23) | copy-start | bytes 49156
  21.1 60.7 %copy-start.1 = (f32[1,3,4096]{2,0,1:T(1,128)S(1)}, f32[1,3,4096]{2,0,1:T(1,128)}, u32[]{:S(2)}) copy-start(f32[1,3,4096]{2,0,1:T(1,128)} %param.22) | copy-start | bytes 147460
  21.1 67.5 %copy-start.2 = (s32[1,16]{1,0:T(1,128)S(1)}, s32[1,16]{1,0:T(1,128)}, u32[]{:S(2)}) copy-start(s32[1,16]{1,0:T(1,128)} %param.29) | copy-start | bytes 196
  81.2 9.6 %copy-start.4 = (f32[3]{0:T(128)S(1)}, f32[3]{0:T(128)}, u32[]{:S(2)}) copy-start(f32[3]{0:T(128)} %constant.233.clone) | copy-start | bytes 40
  81.5 7.1 collective-permute-start.2
  89.3 1.5 collective-permute-start.3
  151.4 7.1 collective-permute-start.4
  159.3 1.7 collective-permute-start.5
  221.6 7.1 collective-permute-start.6
  229.4 1.5 collective-permute-start.7
  291.5 7.1 collective-permute-start.8
  299.4 1.5 collective-permute-start.9
  378.2 8.2 %copy-start = (f32[1,3,4096]{2,0,1:T(1,128)S(1)}, f32[1,3,4096]{2,0,1:T(1,128)}, u32[]{:S(2)}) copy-start(f32[1,3,4096]{2,0,1:T(1,128)} %param.21) | copy-start | bytes 147460
  378.4 8.9 %copy-start.5 = (s32[16,2]{0,1:T(2,128)S(1)}, s32[16,2]{0,1:T(2,128)}, u32[]{:S(2)}) copy-start(s32[16,2]{0,1:T(2,128)} %param.30) | copy-start | bytes 388
  378.5 7.3 collective-permute-start.10
Sparse Core Ops, SparseCore 0:
  387.4 374.6 all-gather.3
where the time goes:
time: 778 us; the launch traced here: 776 us
  waiting for transfers between devices  397 us (51%)
  other arithmetic  204 us (26%)
  matrix products  91.9 us (12%)
  local copies, waits for them, and re-layouts  31.6 us (4%)
  between operations  18.9 us (2%)
  loops' own time  12.9 us (2%)
  blocking collectives  10.9 us (1%)
  starting transfers between devices  8.55 us (1%)
    all_gather x1, waiting for transfers between devices, local(): shard_rows = lax.all_gather(state[None], 'rep', axis=0, tiled=True)  359 us
    mul x108, other arithmetic, pair_block(): pushes = (2.0 * slope * weight_col)[None, :, :] * offsets  89 us
    reduce_sum x60, other arithmetic, pair_block(): force_j = -pushes.sum(1).reshape(3, count_tiles, CL)  56.1 us
    ppermute x11, waiting for transfers between devices, from_behind(): return lax.ppermute(value, axis, pairs)  37.5 us
    sub x60, other arithmetic, pair_block(): coords_i[:, :, :, None] - coords_j[:, None, :, :]  28.5 us
    reduce_sum x12, other arithmetic, pair_block(): jnp.sum(jnp.where(self_pair, 0.0, (gauss_term + coulomb) * weight_col))  21.4 us
    dot_general x60, matrix products, pair_block(): jnp.einsum('te,xtc->xec', select_second, force_j, precision=exact)  18.1 us
    dot_general x60, matrix products, pair_block(): jnp.einsum('te,xec->xtc', select_second, extended, precision=exact)  17.7 us
  transfers between devices with their start and end apart: 12, of which 10 were waited for; matrix products, arithmetic and copies ran while one was open for 1% of the time, Pallas kernels for 0%

commit v1 on v0

--- a/solution.py
+++ b/solution.py
@@ -151,7 +151,15 @@
     potential = (total_energy / (atoms_here * lax.axis_size("slab"))).reshape(1)
     state = jnp.concatenate([coords, speeds], 0)
     partner_me = partner_of(swap_pairs, lax.axis_index("rep").reshape(1))[0]
-    shard_rows = lax.all_gather(state[None], "rep", axis=0, tiled=True)
+    shard_rows = jnp.concatenate(
+        lax.all_to_all(
+            jnp.stack(lax.axis_size("rep") * [state[None]]),
+            split_axis=0,
+            concat_axis=0,
+            axis_name="rep",
+        ),
+        0,
+    )
     row_ids = jnp.arange(shard_rows.shape[0], dtype=jnp.int32)
     chosen = row_ids == partner_me
     swapped = jnp.sum(jnp.where(chosen[:, None, None], shard_rows, 0.0), 0)

time: 778 us -> 547 us (0.70)
  waiting for transfers between devices: 397 us -> 69.8 us
  blocking collectives: 10.9 us -> 101 us
  between operations: 18.9 us -> 5.55 us
  starting transfers between devices: 8.55 us -> 18.2 us
  other arithmetic: 204 us -> 212 us
    all_gather x1 -> x0, waiting for transfers between devices: 359 us -> none  [local(): shard_rows = lax.all_gather(state[None], 'rep', axis=0, tiled=True)]
    psum x1, blocking collectives: 10.9 us -> 101 us  [local(): total_energy = lax.psum(energy, 'slab')]
    all_to_all x0 -> x1, waiting for transfers between devices: none -> 32.4 us  [local(): lax.all_to_all(jnp.stack(lax.axis_size('rep') * [state[None]]), split_axi...]
    all_to_all x0 -> x1, starting transfers between devices: none -> 9.64 us  [local(): lax.all_to_all(jnp.stack(lax.axis_size('rep') * [state[None]]), split_axi...]
where the time goes in v1:
time: 547 us; the launch traced here: 544 us
  other arithmetic  212 us (39%)
  blocking collectives  101 us (18%)
  matrix products  85.9 us (16%)
  waiting for transfers between devices  69.8 us (13%)
  local copies, waits for them, and re-layouts  38.3 us (7%)
  starting transfers between devices  18.2 us (3%)
  loops' own time  13.2 us (2%)
  between operations  5.55 us (1%)
    psum x1, blocking collectives, local(): total_energy = lax.psum(energy, 'slab')  101 us
    mul x108, other arithmetic, pair_block(): pushes = (2.0 * slope * weight_col)[None, :, :] * offsets  91.2 us
    reduce_sum x60, other arithmetic, pair_block(): force_j = -pushes.sum(1).reshape(3, count_tiles, CL)  56.2 us
    ppermute x11, waiting for transfers between devices, from_behind(): return lax.ppermute(value, axis, pairs)  37.4 us
    all_to_all x1, waiting for transfers between devices, local(): lax.all_to_all(jnp.stack(lax.axis_size('rep') * [state[None]]), split_axi...  32.4 us
    sub x60, other arithmetic, pair_block(): coords_i[:, :, :, None] - coords_j[:, None, :, :]  29.5 us
    reduce_sum x12, other arithmetic, pair_block(): jnp.sum(jnp.where(self_pair, 0.0, (gauss_term + coulomb) * weight_col))  21.4 us
    dot_general x60, matrix products, pair_block(): jnp.einsum('te,xtc->xec', select_second, force_j, precision=exact)  18 us
  transfers between devices with their start and end apart: 12, of which 10 were waited for; matrix products, arithmetic and copies ran while one was open for 1% of the time, Pallas kernels for 0%

profile of v1, /device:TPU:0, one launch (start us, length us, event | category | flops | bytes accessed | tf_op | source)
XLA Modules:
  0.0 544.4 jit_solution(176474316247181587)
XLA Ops:
  3.1 4.9 collective-permute-start
  14.6 60.1 %while.67 = (s32[]{:T(128)}, f32[3,80,64]{1,2,0:T(8,128)S(1)}, s32[12,16]{1,0:T(8,128)S(1)}, f32[2,80,64]{1,2,0:T(8,128)S(1)}, s32[12,16]{1,0:T(8,128)S(1)}, /*i...) while((s32[]{:T(128)}, f32[3,80,64]{1,2,0:T(8,128)S(1)}, ...), condition=%wide.region_7.8_spmd.clone, body=%wide.region_4.7_spmd.clone.sunk | while | flops 17876564 | bytes 2778051 | solution.py:135
  17.0 1.1 fusion.307
  22.0 1.1 fusion.307
  27.0 1.1 fusion.307
  32.0 1.1 fusion.307
  37.0 1.1 fusion.307
  42.0 1.1 fusion.307
  47.0 1.1 fusion.307
  52.0 1.1 fusion.307
  57.1 1.1 fusion.307
  62.1 1.1 fusion.307
  67.1 1.1 fusion.307
  72.1 1.1 fusion.307
  75.6 6.4 %collective-permute-done.2 = f32[3,1024]{1,0:T(4,128)S(1)} collective-permute-done((f32[3,1024]{1,0:T(4,128)S(1)}, f32[3,1024]{1,0:T(4,128)S(1)}, u32[]{:S(2)}, u32[]{:S(2)}) %collective-permute-start.2) | collective-permute-done | bytes 12320 | tf_op jit(solution)/shard_map/ppermute | solution.py:22
  82.8 1.4 collective-permute-done.3
  84.6 60.1 %while.68 = (s32[]{:T(128)}, f32[3,80,64]{1,2,0:T(8,128)S(1)}, s32[12,16]{1,0:T(8,128)S(1)}, f32[2,80,64]{1,2,0:T(8,128)S(1)}, s32[12,16]{1,0:T(8,128)S(1)}, /*i...) while((s32[]{:T(128)}, f32[3,80,64]{1,2,0:T(8,128)S(1)}, ...), condition=%wide.region_11.12_spmd.clone, body=%wide.region_8.11_spmd.clone.sunk | while | flops 17876564 | bytes 2778051 | solution.py:135
  92.1 1.1 fusion.323
  97.1 1.1 fusion.323
  107.1 1.1 fusion.323
  112.1 1.1 fusion.323
  145.5 6.5 %collective-permute-done.4 = f32[3,1024]{1,0:T(4,128)S(1)} collective-permute-done((f32[3,1024]{1,0:T(4,128)S(1)}, f32[3,1024]{1,0:T(4,128)S(1)}, u32[]{:S(2)}, u32[]{:S(2)}) %collective-permute-start.4) | collective-permute-done | bytes 12320 | tf_op jit(solution)/shard_map/ppermute | solution.py:22
  153.0 1.4 collective-permute-done.5
  154.8 60.1 %while.69 = (s32[]{:T(128)}, f32[3,80,64]{1,2,0:T(8,128)S(1)}, s32[12,16]{1,0:T(8,128)S(1)}, f32[2,80,64]{1,2,0:T(8,128)S(1)}, s32[12,16]{1,0:T(8,128)S(1)}, /*i...) while((s32[]{:T(128)}, f32[3,80,64]{1,2,0:T(8,128)S(1)}, ...), condition=%wide.region_15.16_spmd.clone, body=%wide.region_12.15_spmd.clone.sunk | while | flops 17876564 | bytes 2778051 | solution.py:135
  215.8 6.5 %collective-permute-done.6 = f32[3,1024]{1,0:T(4,128)S(1)} collective-permute-done((f32[3,1024]{1,0:T(4,128)S(1)}, f32[3,1024]{1,0:T(4,128)S(1)}, u32[]{:S(2)}, u32[]{:S(2)}) %collective-permute-start.6) | collective-permute-done | bytes 12320 | tf_op jit(solution)/shard_map/ppermute | solution.py:22
  223.1 1.4 collective-permute-done.7
  224.9 60.1 %while.70 = (s32[]{:T(128)}, f32[3,80,64]{1,2,0:T(8,128)S(1)}, s32[12,16]{1,0:T(8,128)S(1)}, f32[2,80,64]{1,2,0:T(8,128)S(1)}, s32[12,16]{1,0:T(8,128)S(1)}, /*i...) while((s32[]{:T(128)}, f32[3,80,64]{1,2,0:T(8,128)S(1)}, ...), condition=%wide.region_19.20_spmd.clone, body=%wide.region_16.19_spmd.clone.sunk | while | flops 17876564 | bytes 2778051 | solution.py:135
  285.8 6.5 %collective-permute-done.8 = f32[3,1024]{1,0:T(4,128)S(1)} collective-permute-done((f32[3,1024]{1,0:T(4,128)S(1)}, f32[3,1024]{1,0:T(4,128)S(1)}, u32[]{:S(2)}, u32[]{:S(2)}) %collective-permute-start.8) | collective-permute-done | bytes 12320 | tf_op jit(solution)/shard_map/ppermute | solution.py:22
  293.1 1.4 collective-permute-done.9
  294.9 77.1 %while.71 = (s32[]{:T(128)}, f32[3,80,64]{1,2,0:T(8,128)S(1)}, f32[]{:T(128)}, s32[12,16]{1,0:T(8,128)S(1)}, f32[2,80,64]{1,2,0:T(8,128)S(1)}, /*index=5*/s32[12...) while((s32[]{:T(128)}, f32[3,80,64]{1,2,0:T(8,128)S(1)}, ...), condition=%wide.region_24.25_spmd.clone, body=%wide.region_20.24_spmd.clone.sunk | while | flops 18283088 | bytes 2786427 | solution.py:135
  297.4 1.8 select_reduce_fusion.2
  303.8 1.8 select_reduce_fusion.2
  310.2 1.8 select_reduce_fusion.2
  316.6 1.8 select_reduce_fusion.2
  323.1 1.8 select_reduce_fusion.2
  329.5 1.8 select_reduce_fusion.2
  335.9 1.8 select_reduce_fusion.2
  342.3 1.8 select_reduce_fusion.2
  348.8 1.8 select_reduce_fusion.2
  355.2 1.8 select_reduce_fusion.2
  361.6 1.8 select_reduce_fusion.2
  368.0 1.8 select_reduce_fusion.2
  373.9 5.7 %collective-permute-done.10 = f32[3,1024]{1,0:T(4,128)S(1)} collective-permute-done((f32[3,1024]{1,0:T(4,128)S(1)}, f32[3,1024]{1,0:T(4,128)S(1)}, u32[]{:S(2)}, u32[]{:S(2)}) %collective-permute-start.10) | collective-permute-done | bytes 12320 | tf_op jit(solution)/shard_map/ppermute | solution.py:22
  380.4 4.4 stack.69
  384.8 9.6 %all-to-all-start = ((f32[64,1,6,4096]{3,1,2,0:T(1,128)}), f32[64,1,6,4096]{3,1,2,0:T(1,128)}, u32[]{:S(2)}, u32[]{:S(2)}) async-start(f32[64,1,6,4096]{3,1,2,0:T(1,128)} %stack.69), calls=%async_computation | async-start | bytes 12582912 | tf_op jit(solution)/shard_map/all_to_all | solution.py:155
  398.3 101.5 %psum.7 = f32[]{:T(128)} all-reduce(f32[]{:T(128)} %get-tuple-element.598), channel_id=1, replica_groups=mesh['rep'=64,'slab'=4] {'slab'}, use_global_device_ids=true, to_apply=%region_26.27 | all-reduce | flops 1 | bytes 8 | tf_op jit(solution)/shard_map/psum | solution.py:150
  500.5 32.4 %all-to-all-done = f32[64,1,6,4096]{3,1,2,0:T(1,128)} async-done(((f32[64,1,6,4096]{3,1,2,0:T(1,128)}), f32[64,1,6,4096]{3,1,2,0:T(1,128)}, u32[]{:S(2)}, u32[]{:S(2)}) %all-to-all-start) | async-done | bytes 6291488 | tf_op jit(solution)/shard_map/all_to_all | solution.py:155
  532.8 9.1 %fusion.130 = f32[6,4096]{1,0:T(8,128)S(1)} fusion(f32[64,1,6,4096]{3,1,2,0:T(1,128)} %all-to-all-done, pred[64]{0:T(512)(128)(4,1)S(1)} %iota_compare_fusion.12), kind=kLoop, calls=%fused_computation.232 | loop fusion | flops 3121152 | bytes 6389824 | tf_op jit(solution)/shard_map/reduce_sum | solution.py:165
  (1011 shorter events, 287.7 us)
Async XLA Ops:
  3.1 10.2 %collective-permute-start = (f32[2,1024]{1,0:T(2,128)S(1)}, f32[2,1024]{1,0:T(2,128)S(1)}, u32[]{:S(2)}, u32[]{:S(2)}) collective-permute-start(f32[2,1024]{1,0:T(2,128)S(1)} %reshape.1066), channel_id=1, source_target_pairs={{0,3},{1,0},{2,1},{3,2},{4,7},{5,4},{6,5},{7,6},{8,11},{9,8},{10,9... | collective-permute-start | bytes 24584 | tf_op jit(solution)/shard_map/ppermute | solution.py:22
  10.1 3.5 collective-permute-start.1
  14.5 60.5 %copy-start.3 = (f32[4096]{0:T(1024)S(1)}, f32[4096]{0:T(1024)}, u32[]{:S(2)}) copy-start(f32[4096]{0:T(1024)} %param.23) | copy-start | bytes 49156
  14.5 60.7 %copy-start.1 = (f32[1,3,4096]{2,0,1:T(1,128)S(1)}, f32[1,3,4096]{2,0,1:T(1,128)}, u32[]{:S(2)}) copy-start(f32[1,3,4096]{2,0,1:T(1,128)} %param.22) | copy-start | bytes 147460
  14.5 67.6 %copy-start.2 = (s32[1,16]{1,0:T(1,128)S(1)}, s32[1,16]{1,0:T(1,128)}, u32[]{:S(2)}) copy-start(s32[1,16]{1,0:T(1,128)} %param.29) | copy-start | bytes 196
  74.7 9.6 %copy-start.4 = (f32[3]{0:T(128)S(1)}, f32[3]{0:T(128)}, u32[]{:S(2)}) copy-start(f32[3]{0:T(128)} %constant.233.clone) | copy-start | bytes 40
  74.9 7.1 %collective-permute-start.2 = (f32[3,1024]{1,0:T(4,128)S(1)}, f32[3,1024]{1,0:T(4,128)S(1)}, u32[]{:S(2)}, u32[]{:S(2)}) collective-permute-start(f32[3,1024]{1,0:T(4,128)S(1)} %reshape.1072), channel_id=1, source_target_pairs={{0,1},{1,2},{2,3},{3,0},{4,5},{5,6},{6,7},{7,4},{8,9},{9,10},{10,1... | collective-permute-start | bytes 36872 | tf_op jit(solution)/shard_map/ppermute | solution.py:22
  82.8 1.5 collective-permute-start.3
  145.0 7.1 %collective-permute-start.4 = (f32[3,1024]{1,0:T(4,128)S(1)}, f32[3,1024]{1,0:T(4,128)S(1)}, u32[]{:S(2)}, u32[]{:S(2)}) collective-permute-start(f32[3,1024]{1,0:T(4,128)S(1)} %reshape.1077), channel_id=1, source_target_pairs={{0,1},{1,2},{2,3},{3,0},{4,5},{5,6},{6,7},{7,4},{8,9},{9,10},{10,1... | collective-permute-start | bytes 36872 | tf_op jit(solution)/shard_map/ppermute | solution.py:22
  152.8 1.7 collective-permute-start.5
  215.2 7.1 %collective-permute-start.6 = (f32[3,1024]{1,0:T(4,128)S(1)}, f32[3,1024]{1,0:T(4,128)S(1)}, u32[]{:S(2)}, u32[]{:S(2)}) collective-permute-start(f32[3,1024]{1,0:T(4,128)S(1)} %reshape.1082), channel_id=1, source_target_pairs={{0,1},{1,2},{2,3},{3,0},{4,5},{5,6},{6,7},{7,4},{8,9},{9,10},{10,1... | collective-permute-start | bytes 36872 | tf_op jit(solution)/shard_map/ppermute | solution.py:22
  223.0 1.5 collective-permute-start.7
  285.2 7.1 %collective-permute-start.8 = (f32[3,1024]{1,0:T(4,128)S(1)}, f32[3,1024]{1,0:T(4,128)S(1)}, u32[]{:S(2)}, u32[]{:S(2)}) collective-permute-start(f32[3,1024]{1,0:T(4,128)S(1)} %reshape.1087), channel_id=1, source_target_pairs={{0,1},{1,2},{2,3},{3,0},{4,5},{5,6},{6,7},{7,4},{8,9},{9,10},{10,1... | collective-permute-start | bytes 36872 | tf_op jit(solution)/shard_map/ppermute | solution.py:22
  293.0 1.5 collective-permute-start.9
  372.0 8.2 %copy-start = (f32[1,3,4096]{2,0,1:T(1,128)S(1)}, f32[1,3,4096]{2,0,1:T(1,128)}, u32[]{:S(2)}) copy-start(f32[1,3,4096]{2,0,1:T(1,128)} %param.21) | copy-start | bytes 147460
  372.3 7.3 %collective-permute-start.10 = (f32[3,1024]{1,0:T(4,128)S(1)}, f32[3,1024]{1,0:T(4,128)S(1)}, u32[]{:S(2)}, u32[]{:S(2)}) collective-permute-start(f32[3,1024]{1,0:T(4,128)S(1)} %reshape.1092), channel_id=1, source_target_pairs={{0,1},{1,2},{2,3},{3,0},{4,5},{5,6},{6,7},{7,4},{8,9},{9,10},{10,1... | collective-permute-start | bytes 36872 | tf_op jit(solution)/shard_map/ppermute | solution.py:22
  384.8 9.7 %copy-start.5 = (s32[16,2]{0,1:T(2,128)S(1)}, s32[16,2]{0,1:T(2,128)}, u32[]{:S(2)}) copy-start(s32[16,2]{0,1:T(2,128)} %param.30) | copy-start | bytes 388
  384.8 148.1 %all-to-all-start = ((f32[64,1,6,4096]{3,1,2,0:T(1,128)}), f32[64,1,6,4096]{3,1,2,0:T(1,128)}, u32[]{:S(2)}, u32[]{:S(2)}) async-start(f32[64,1,6,4096]{3,1,2,0:T(1,128)} %stack.69), calls=%async_computation | async-start | bytes 12582912 | tf_op jit(solution)/shard_map/all_to_all | solution.py:155
